TPU v7x, 32 devices: a whole 2x2x4 slice. The times are simulated.
32 devices in a mesh: parts: 2 (over y), req: 8 (over z, x), mp: 2 (over core).
Axes of the slice: x: 2, y: 2, z: 4, core: 2. Of those that a mesh axis runs over, the one named last changes fastest.
Arguments:
- hidden: bfloat16 [2048, 8192], P(('parts', 'req'), 'mp'), parts along dimension 0, may hold values from -6 to 6
- base_query_block: bfloat16 [2048, 1024], P(('parts', 'req'), 'mp'), parts along dimension 0, may hold values from -112 to 112
- key_value_block: bfloat16 [2048, 256], P(('parts', 'req')), parts along dimension 0, may hold values from -7.1875 to 7.1875
- prefix_page_store: bfloat16 [256, 32, 256], P(('parts', 'req')), parts along dimension 0, may hold values from -8 to 8
- adapter_down_weight: bfloat16 [8, 2, 64, 4096], P('req', 'mp'), may hold values from -0.0625 to 0.0625
- adapter_up_weight: bfloat16 [8, 2, 64, 512], P('req', 'mp'), may hold values from -0.75 to 0.75
- request_adapter: int32 [16], P(('parts', 'req')), parts along dimension 0, may hold values from 0 to 7
- prefix_page_count: int32 [16], P(('parts', 'req')), parts along dimension 0, may hold values from 2 to 8, as said below
- page_owner_groups: int32 [16, 8], P(('parts', 'req')), parts along dimension 0, may hold values from 0 to 7, as said below
- page_pool_row: int32 [16, 8], P(('parts', 'req')), parts along dimension 0, may hold values from 0 to 15
Outputs:
- attn_out: bfloat16 [2048, 1024], P(('parts', 'req'), 'mp'), parts along dimension 0
There are 2 independent parts, one for each index of `parts`. A program takes and returns all parts, laid end to end along the dimension named above; an argument that names none is the same for every part. Nothing has to cross between parts.
Inputs may be any that keep to these rules, and one draw needn't show every extreme that they name: `prefix_page_count`: some request has exactly 8 prefix pages. `page_owner_groups`: each row names every request group once; its first prefix_page_count[r] entries hold request r's prefix pages, the rest is padding.
All inputs are finite; a program needn't handle non-finite values.
Results may differ from a plain program's by a relative error of at most 0.025.
Values may be sent and summed in bfloat16 or wider, within the bound.
No kernel may reach another device: no remote copies, remote signals or barrier semaphores. Data moves between devices by JAX's collectives and lax.ppermute only.
A program may use at most 64 MiB of HBM per device.

v0:
```python
import math
import jax
import jax.numpy as jnp
from jax import lax
from jax.sharding import PartitionSpec as P

ROPE_BASE = 500000.0
LANES = 128
TILE_ROWS = 16


def rotate(vectors, positions):
    head_width = vectors.shape[-1]
    half_dim = head_width // 2
    frequency = ROPE_BASE ** (-2.0 * jnp.arange(half_dim, dtype=jnp.float32) / head_width)
    angles = positions.astype(jnp.float32)[:, None] * frequency[None, :]
    cosine = jnp.concatenate([jnp.cos(angles), jnp.cos(angles)], axis=1)[:, None, :]
    sine_part = jnp.concatenate([jnp.sin(angles), jnp.sin(angles)], axis=1)[:, None, :]
    turned = jnp.concatenate([-vectors[..., half_dim:], vectors[..., :half_dim]], axis=-1)
    return vectors * cosine + turned * sine_part


def tiled_ok(shape, groups):
    rows, cols = shape
    if rows % TILE_ROWS or cols % LANES:
        return False
    return rows // TILE_ROWS * (cols // LANES) % groups == 0


def to_pieces(matrix, groups):
    rows, cols = matrix.shape
    if tiled_ok(matrix.shape, groups):
        tiles = matrix.reshape(rows // TILE_ROWS, TILE_ROWS, cols // LANES, LANES)
        tiles = jnp.transpose(tiles, (0, 2, 1, 3))
        return tiles.reshape(groups, -1, LANES)
    flat = matrix.reshape(groups, -1)
    extra = -flat.shape[1] % LANES
    if extra:
        flat = jnp.pad(flat, ((0, 0), (0, extra)))
    return flat.reshape(groups, -1, LANES)


def from_pieces(pieces, shape):
    rows, cols = shape
    groups = pieces.shape[0]
    if tiled_ok(shape, groups):
        tiles = pieces.reshape(rows // TILE_ROWS, cols // LANES, TILE_ROWS, LANES)
        tiles = jnp.transpose(tiles, (0, 2, 1, 3))
        return tiles.reshape(rows, cols)
    flat = pieces.reshape(groups, -1)[:, : rows * cols // groups]
    return flat.reshape(rows, cols)


def piece_rows(shape, groups):
    rows, cols = shape
    if tiled_ok(shape, groups):
        return rows * cols // groups // LANES
    return -(-(rows * cols // groups) // LANES)


def attend(queries, all_keys, all_values, allowed):
    token_count, head_count, head_width = queries.shape
    score_scale = 1.0 / math.sqrt(head_width)
    rows = queries.reshape(token_count * head_count, head_width)
    scores = (
        lax.dot_general(
            rows, all_keys, (((1,), (1,)), ((), ())), preferred_element_type=jnp.float32
        )
        * score_scale
    )
    scores = scores.reshape(token_count, head_count, -1)
    scores = jnp.where(allowed[:, None, :], scores, -jnp.inf)
    row_max = jnp.max(scores, axis=2, keepdims=True)
    weights = jnp.exp(scores - row_max)
    weights_bf = (weights / jnp.sum(weights, axis=2, keepdims=True)).astype(jnp.bfloat16)
    out = jnp.dot(
        weights_bf.reshape(token_count * head_count, -1),
        all_values,
        preferred_element_type=jnp.float32,
    ).astype(jnp.bfloat16)
    return out.reshape(token_count, head_count * head_width)


def on_device(
    hidden,
    base_query_block,
    key_value_block,
    prefix_page_store,
    adapter_down_weight,
    adapter_up_weight,
    request_adapter,
    prefix_page_count,
    page_owner_groups,
    page_pool_row,
):
    groups = lax.axis_size("req")
    head_width = key_value_block.shape[1] // 2
    total_row_count = hidden.shape[0]
    page_len = prefix_page_store.shape[1]
    held = adapter_down_weight.shape[0]
    down_shape = adapter_down_weight.shape[2:]
    up_shape = adapter_up_weight.shape[2:]
    down_rows = piece_rows(down_shape, groups)
    up_rows = piece_rows(up_shape, groups)
    page_count = prefix_page_count[0]
    slot_order = jnp.arange(page_owner_groups.shape[1], dtype=jnp.int32)
    live_slots = slot_order < page_count
    holder_order = jnp.arange(groups, dtype=jnp.int32)
    matched = (page_owner_groups[0][None, :] == holder_order[:, None]) & live_slots[None, :]
    wanted = jnp.max(jnp.where(matched, page_pool_row[0][None, :], -1), axis=1)
    asks = jnp.zeros((groups, 1, LANES), jnp.float32)
    asks = asks.at[:, 0, 0].set(jnp.maximum(wanted, 0).astype(jnp.float32))
    asks = asks.at[:, 0, 1].set(request_adapter[0].astype(jnp.float32))
    parts_out = []
    for a in range(held):
        parts_out.append(to_pieces(adapter_down_weight[a, 0], groups))
        parts_out.append(to_pieces(adapter_up_weight[a, 0], groups))
    parts_out.append(asks.astype(jnp.bfloat16))
    stage_one = jnp.concatenate(parts_out, axis=1)
    stage_one = lax.all_to_all(stage_one, "req", split_axis=0, concat_axis=0, tiled=True)
    share_rows = down_rows + up_rows
    shares = stage_one[:, : held * share_rows].reshape(groups * held, share_rows, LANES)
    their_asks = stage_one[:, held * share_rows, :2].astype(jnp.int32)
    their_pages = their_asks[:, 0]
    their_adapters = their_asks[:, 1]
    picked = jnp.take(shares, their_adapters, axis=0)
    pages = jnp.take(prefix_page_store, their_pages, axis=0)
    page_pieces = jax.vmap(lambda page: to_pieces(page, 1)[0])(pages)
    stage_two = jnp.concatenate([picked, page_pieces], axis=1)
    stage_two = lax.all_to_all(stage_two, "req", split_axis=0, concat_axis=0, tiled=True)
    down_projected_rows = from_pieces(stage_two[:, :down_rows], down_shape)
    up_projected_rows = from_pieces(stage_two[:, down_rows:share_rows], up_shape)
    fetched = jax.vmap(lambda piece: from_pieces(piece[None], (page_len, 2 * head_width)))(
        stage_two[:, share_rows:]
    )
    partial_value = lax.dot_general(
        hidden, down_projected_rows, (((1,), (1,)), ((), ())), preferred_element_type=jnp.float32
    )
    rank_reduce = lax.psum(partial_value, "mp").astype(jnp.bfloat16)
    adapter_delta = jnp.dot(rank_reduce, up_projected_rows, preferred_element_type=jnp.float32)
    query_head_count = base_query_block.shape[1] // head_width
    positions = page_len * page_count + jnp.arange(total_row_count, dtype=jnp.int32)
    reduced_sum = (base_query_block.astype(jnp.float32) + adapter_delta).reshape(
        total_row_count, query_head_count, head_width
    )
    queries = rotate(reduced_sum, positions).astype(jnp.bfloat16)
    block_keys = rotate(key_value_block[:, None, :head_width].astype(jnp.float32), positions)[
        :, 0
    ].astype(jnp.bfloat16)
    flat_pages = fetched.reshape(groups * page_len, 2 * head_width)
    prefix_mask = jnp.repeat(wanted >= 0, page_len)
    all_keys = jnp.concatenate([flat_pages[:, :head_width], block_keys], axis=0)
    all_values = jnp.concatenate(
        [flat_pages[:, head_width:], key_value_block[:, head_width:]], axis=0
    )
    token_order = jnp.arange(total_row_count, dtype=jnp.int32)
    causal = token_order[:, None] >= token_order[None, :]
    allowed = jnp.concatenate(
        [jnp.broadcast_to(prefix_mask[None, :], (total_row_count, groups * page_len)), causal],
        axis=1,
    )
    return attend(queries, all_keys, all_values, allowed)


def solution(mesh):
    in_specs = (
        P(("parts", "req"), "mp"),
        P(("parts", "req"), "mp"),
        P(("parts", "req"), None),
        P(("parts", "req"), None, None),
        P("req", "mp", None, None),
        P("req", "mp", None, None),
        P(("parts", "req")),
        P(("parts", "req")),
        P(("parts", "req"), None),
        P(("parts", "req"), None),
    )
    out_specs = P(("parts", "req"), "mp")
    return jax.shard_map(
        on_device, mesh=mesh, in_specs=in_specs, out_specs=out_specs, check_vma=False
    )
```

profile of v0, /device:TPU:0, one launch (start us, length us, event | category | flops | bytes accessed | tf_op | source)
XLA Modules:
  0.0 64.4 jit_solution(6399788822573083362)
XLA Ops:
  0.0 0.0 copy-start
  0.8 0.8 %select_reduce_fusion = s32[8]{0:T(128)S(1)} fusion(s32[8]{0:T(128)} %bitcast.92, s32[8]{0:T(128)} %bitcast.93, pred[8]{0:T(512)(128)(4,1)S(1)} %iota_compare_fusion.2), kind=kLoop, calls=%fused_computation.48 | loop fusion | flops 248 | bytes 104 | tf_op jit(solution)/shard_map/reduce_max | solution.py:110
  1.6 0.1 copy.78
  2.3 0.7 %slice.88 = s32[1]{0:T(128)} slice(s32[2]{0:T(128)S(1)} %iota.33), slice={[1:2]} | slice | bytes 8 | tf_op jit(solution)/shard_map/slice.52
  3.0 1.1 %copy.90 = bf16[8,8,32,128]{3,2,1,0:T(8,128)(2,1)S(1)} copy(bf16[8,8,32,128]{3,1,2,0:T(8,128)(2,1)} %bitcast.84) | data formatting | bytes 1048576
  4.1 0.0 copy-start.4
  4.2 0.2 copy.76
  4.4 0.6 copy-done.4
  5.0 1.3 %scatter.9 = bf16[8,1,128]{2,1,0:T(2,128)(2,1)S(1)} dynamic-update-slice(bf16[8,1,128]{2,1,0:T(2,128)(2,1)S(1)} %scatter.6, bf16[8,1,1]{2,1,0:T(2,128)(2,1)S(1)} %broadcast.132, s32[]{:T(128)} %constant.94.clone.1, s32[]{:T(128)} %constant.94.clone.1, s32[]{:T(128)} %bitcast.9) | dynamic-update-slice | bytes 36 | tf_op jit(solution)/shard_map/scatter | solution.py:113
  6.4 0.9 %pad_maximum_fusion.1 = bf16[8,289,128]{2,1,0:T(8,128)(2,1)} fusion(bf16[8,1,128]{2,1,0:T(2,128)(2,1)S(1)} %scatter.9, bf16[8,32,128]{2,1,0:T(8,128)(2,1)S(1)} %bitcast.88, bf16[8,256,128]{2,1,0:T(8,128)(2,1)S(1)} %bitcast.76), kind=kLoop, calls=%fused_computation.12 | loop fusion | flops 1775616 | bytes 1183744 | tf_op jit(solution)/shard_map/concatenate | solution.py:119
  7.2 7.3 %all-to-all-start = ((bf16[8,289,128]{2,1,0:T(8,128)(2,1)}), bf16[8,289,128]{2,1,0:T(8,128)(2,1)S(1)}, u32[]{:S(2)}, u32[]{:S(2)}) async-start(bf16[8,289,128]{2,1,0:T(8,128)(2,1)} %pad_maximum_fusion.1), calls=%async_computation | async-start | bytes 1212416 | tf_op jit(solution)/shard_map/all_to_all | solution.py:120
  14.5 0.1 broadcast_in_dim.82
  14.6 0.1 reshape.188
  14.7 16.0 %all-to-all-done = bf16[8,289,128]{2,1,0:T(8,128)(2,1)S(1)} async-done(((bf16[8,289,128]{2,1,0:T(8,128)(2,1)}), bf16[8,289,128]{2,1,0:T(8,128)(2,1)S(1)}, u32[]{:S(2)}, u32[]{:S(2)}) %all-to-all-start) | async-done | bytes 591904 | tf_op jit(solution)/shard_map/all_to_all | solution.py:120
  30.7 0.1 copy.88
  30.9 0.0 copy-start.3
  30.9 0.4 copy.89
  31.3 0.5 copy-done.3
  31.8 0.6 gather_fusion.1
  32.4 0.2 fusion.7
  32.6 0.2 copy.82
  32.8 0.7 %gather_fusion = bf16[8,288,128]{1,2,0:T(8,128)(2,1)S(1)} fusion(bf16[8,288,128]{1,2,0:T(8,128)(2,1)S(1)} %copy.89, s32[1024]{0:T(1024)S(1)} %get-tuple-element.49), kind=kCustom, calls=%fused_computation | custom fusion | bytes 1179680 | tf_op jit(solution)/shard_map/jit(_take)/gather | solution.py:126
  33.6 0.2 broadcast_select_fusion
  33.7 0.2 pad_maximum_fusion
  33.9 1.1 %copy.83 = bf16[8,352,128]{2,1,0:T(8,128)(2,1)} copy(bf16[8,352,128]{1,2,0:T(8,128)(2,1)S(1)} %pad_maximum_fusion) | data formatting | bytes 1441792 | tf_op jit(solution)/shard_map/concatenate | solution.py:129
  35.0 0.0 copy-start.1
  35.0 3.8 %all-to-all-start.1 = ((bf16[8,352,128]{2,1,0:T(8,128)(2,1)}), bf16[8,352,128]{2,1,0:T(8,128)(2,1)S(1)}, u32[]{:S(2)}, u32[]{:S(2)}) async-start(bf16[8,352,128]{2,1,0:T(8,128)(2,1)} %copy.83), calls=%async_computation.1 | async-start | bytes 1441792 | tf_op jit(solution)/shard_map/all_to_all | solution.py:130
  38.8 0.2 broadcast_in_dim.85
  39.0 0.2 broadcast_in_dim.86
  39.2 0.3 copy.87
  39.5 0.0 copy-done.1
  39.5 0.3 multiply_cosine_fusion
  39.8 0.1 fusion.18
  39.9 0.1 fusion.15
  40.1 17.7 %all-to-all-done.1 = bf16[8,352,128]{2,1,0:T(8,128)(2,1)S(1)} async-done(((bf16[8,352,128]{2,1,0:T(8,128)(2,1)}), bf16[8,352,128]{2,1,0:T(8,128)(2,1)S(1)}, u32[]{:S(2)}, u32[]{:S(2)}) %all-to-all-start.1) | async-done | bytes 720928 | tf_op jit(solution)/shard_map/all_to_all | solution.py:130
  57.8 0.1 copy.84
  57.9 0.0 copy-start.2
  57.9 0.0 copy-done
  57.9 0.5 convolution_bitcast_fusion
  58.4 3.4 %psum.7 = bf16[128,64]{0,1:T(8,128)(2,1)S(1)} all-reduce(f32[128,64]{0,1:T(8,128)S(1)} %convolution_bitcast_fusion), channel_id=1, replica_groups=mesh['parts'=2,'req'=8,'mp'=2] {'mp'}, use_global_device_ids=true, to_apply=%region_1.2 | all-reduce | flops 8192 | bytes 49152 | tf_op jit(solution)/shard_map/psum | solution.py:139
  61.9 0.0 copy-done.2
  61.9 0.2 convolution_add_fusion
  62.1 0.1 reshape.168
  62.2 0.2 slice_negate_fusion
  62.5 0.1 copy.86
  62.7 0.4 fusion.28
  63.2 0.2 fusion.1
  63.3 0.3 convolution_convert_fusion
  63.6 0.7 %reshape.170 = bf16[128,512]{1,0:T(8,128)(2,1)} reshape(bf16[512,128]{1,0:T(8,128)(2,1)S(1)} %convolution_convert_fusion) | data formatting | bytes 262144 | tf_op jit(solution)/shard_map/reshape | solution.py:81
  (32 shorter events, 0.5 us)
Async XLA Ops:
  0.0 57.9 %copy-start = (bf16[128,4096]{1,0:T(8,128)(2,1)S(1)}, bf16[128,4096]{1,0:T(8,128)(2,1)}, u32[]{:S(2)}) copy-start(bf16[128,4096]{1,0:T(8,128)(2,1)} %param.14) | copy-start | bytes 3145732
  4.1 0.8 %copy-start.4 = (bf16[1,1,64,512]{3,2,1,0:T(8,128)(2,1)S(1)}, bf16[1,1,64,512]{3,2,1,0:T(8,128)(2,1)}, u32[]{:S(2)}) copy-start(bf16[1,1,64,512]{3,2,1,0:T(8,128)(2,1)} %param.19) | copy-start | bytes 196612
  7.2 23.5 %all-to-all-start = ((bf16[8,289,128]{2,1,0:T(8,128)(2,1)}), bf16[8,289,128]{2,1,0:T(8,128)(2,1)S(1)}, u32[]{:S(2)}, u32[]{:S(2)}) async-start(bf16[8,289,128]{2,1,0:T(8,128)(2,1)} %pad_maximum_fusion.1), calls=%async_computation | async-start | bytes 1212416 | tf_op jit(solution)/shard_map/all_to_all | solution.py:120
  30.9 1.0 %copy-start.3 = (bf16[16,32,256]{2,1,0:T(8,128)(2,1)S(1)}, bf16[16,32,256]{2,1,0:T(8,128)(2,1)}, u32[]{:S(2)}) copy-start(bf16[16,32,256]{2,1,0:T(8,128)(2,1)} %param.17) | copy-start | bytes 786436
  35.0 4.5 %copy-start.1 = (bf16[128,256]{1,0:T(8,128)(2,1)S(1)}, bf16[128,256]{1,0:T(8,128)(2,1)}, u32[]{:S(2)}) copy-start(bf16[128,256]{1,0:T(8,128)(2,1)} %param.16) | copy-start | bytes 196612
  35.0 22.7 %all-to-all-start.1 = ((bf16[8,352,128]{2,1,0:T(8,128)(2,1)}), bf16[8,352,128]{2,1,0:T(8,128)(2,1)S(1)}, u32[]{:S(2)}, u32[]{:S(2)}) async-start(bf16[8,352,128]{2,1,0:T(8,128)(2,1)} %copy.83), calls=%async_computation.1 | async-start | bytes 1441792 | tf_op jit(solution)/shard_map/all_to_all | solution.py:130
  57.9 4.0 %copy-start.2 = (bf16[128,512]{1,0:T(8,128)(2,1)S(1)}, bf16[128,512]{1,0:T(8,128)(2,1)}, u32[]{:S(2)}) copy-start(bf16[128,512]{1,0:T(8,128)(2,1)} %param.15) | copy-start | bytes 393220
where the time goes:
time: 64.9 us; the launch traced here: 64.4 us
  waiting for transfers between devices  33.7 us (52%)
  starting transfers between devices  11 us (17%)
  local copies, waits for them, and re-layouts  9.87 us (15%)
  blocking collectives  3.41 us (5%)
  other arithmetic  3.15 us (5%)
  between operations  1.79 us (3%)
  matrix products  1.43 us (2%)
    all_to_all x1, waiting for transfers between devices, on_device(): lax.all_to_all(stage_two, 'req', split_axis=0, concat_axis=0, tiled=True)  17.7 us
    all_to_all x1, waiting for transfers between devices, on_device(): lax.all_to_all(stage_one, 'req', split_axis=0, concat_axis=0, tiled=True)  16 us
    all_to_all x1, starting transfers between devices, on_device(): lax.all_to_all(stage_one, 'req', split_axis=0, concat_axis=0, tiled=True)  7.25 us
    all_to_all x1, starting transfers between devices, on_device(): lax.all_to_all(stage_two, 'req', split_axis=0, concat_axis=0, tiled=True)  3.77 us
    psum x1, blocking collectives, on_device(): rank_reduce = lax.psum(partial_value, 'mp').astype(jnp.bfloat16)  3.41 us
    unnamed x14, local copies, waits for them, and re-layouts  2.72 us
    scatter x1, local copies, waits for them, and re-layouts, on_device(): asks = asks.at[:, 0, 1].set(request_adapter[0].astype(jnp.float32))  1.33 us
  transfers between devices with their start and end apart: 2, of which 2 were waited for; matrix products, arithmetic and copies ran while one was open for 2% of the time, Pallas kernels for 0%

commit v1 on v0

--- a/solution.py
+++ b/solution.py
@@ -7,6 +7,17 @@
 ROPE_BASE = 500000.0
 LANES = 128
 TILE_ROWS = 16
+
+
+def cut_along(x, dim, size):
+    before, after = (x.shape[:dim], x.shape[dim + 1 :])
+    return jnp.moveaxis(x.reshape(*before, size, -1, *after), dim, 0)
+
+
+def in_order(blocks, dim):
+    lengths = list(blocks.shape[1:])
+    lengths[dim] *= blocks.shape[0]
+    return jnp.moveaxis(blocks, 0, dim).reshape(lengths)
 
 
 def rotate(vectors, positions):
@@ -117,7 +128,14 @@
         parts_out.append(to_pieces(adapter_up_weight[a, 0], groups))
     parts_out.append(asks.astype(jnp.bfloat16))
     stage_one = jnp.concatenate(parts_out, axis=1)
-    stage_one = lax.all_to_all(stage_one, "req", split_axis=0, concat_axis=0, tiled=True)
+    size, index = (lax.axis_size("req"), lax.axis_index("req"))
+    parts = cut_along(stage_one, 0, size)
+    finished = [parts[index]]
+    for step in range(1, size):
+        sent = parts[index ^ step]
+        finished.append(lax.ppermute(sent, "req", [(i, i ^ step) for i in range(size)]))
+    parts = jnp.stack(finished)[index ^ jnp.arange(size)]
+    stage_one = in_order(parts, 0)
     share_rows = down_rows + up_rows
     shares = stage_one[:, : held * share_rows].reshape(groups * held, share_rows, LANES)
     their_asks = stage_one[:, held * share_rows, :2].astype(jnp.int32)

time: 64.9 us -> 62.5 us (0.963)
  waiting for transfers between devices: 33.7 us -> 24.5 us
  starting transfers between devices: 11 us -> 18 us
  other arithmetic: 3.15 us -> 2.33 us
    all_to_all x1 -> x0, waiting for transfers between devices: 16 us -> none  [on_device(): lax.all_to_all(stage_one, 'req', split_axis=0, concat_axis=0, tiled=True)]
    ppermute x0 -> x7, starting transfers between devices: none -> 12.6 us  [on_device(): lax.ppermute(sent, 'req', [(i, i ^ step) for i in range(size)])]
    all_to_all x1 -> x0, starting transfers between devices: 7.25 us -> none  [on_device(): lax.all_to_all(stage_one, 'req', split_axis=0, concat_axis=0, tiled=True)]
    ppermute x0 -> x7, waiting for transfers between devices: none -> 7.04 us  [on_device(): lax.ppermute(sent, 'req', [(i, i ^ step) for i in range(size)])]
    all_to_all x1, starting transfers between devices: 3.77 us -> 5.41 us  [on_device(): lax.all_to_all(stage_two, 'req', split_axis=0, concat_axis=0, tiled=True)]
    concatenate x1, other arithmetic: 0.87 us -> 0.04 us  [on_device(): stage_one = jnp.concatenate(parts_out, axis=1)]
    gather x0 -> x1, local copies, waits for them, and re-layouts: none -> 0.67 us  [on_device(): parts = jnp.stack(finished)[index ^ jnp.arange(size)]]
    unnamed x14 -> x20, local copies, waits for them, and re-layouts: 2.72 us -> 2.32 us
  transfers between devices with their start and end apart: 2 -> 8, of which waited for: 2 -> 3; matrix products, arithmetic and copies ran while one was open for 2% -> 2% of each run, Pallas kernels for 0% -> 0%
where the time goes in v1:
time: 62.5 us; the launch traced here: 62.1 us
  waiting for transfers between devices  24.5 us (39%)
  starting transfers between devices  18 us (29%)
  local copies, waits for them, and re-layouts  10.5 us (17%)
  blocking collectives  3.41 us (5%)
  other arithmetic  2.33 us (4%)
  between operations  1.94 us (3%)
  matrix products  1.43 us (2%)
    all_to_all x1, waiting for transfers between devices, on_device(): lax.all_to_all(stage_two, 'req', split_axis=0, concat_axis=0, tiled=True)  17.5 us
    ppermute x7, starting transfers between devices, on_device(): lax.ppermute(sent, 'req', [(i, i ^ step) for i in range(size)])  12.6 us
    ppermute x7, waiting for transfers between devices, on_device(): lax.ppermute(sent, 'req', [(i, i ^ step) for i in range(size)])  7.04 us
    all_to_all x1, starting transfers between devices, on_device(): lax.all_to_all(stage_two, 'req', split_axis=0, concat_axis=0, tiled=True)  5.41 us
    psum x1, blocking collectives, on_device(): rank_reduce = lax.psum(partial_value, 'mp').astype(jnp.bfloat16)  3.41 us
    unnamed x20, local copies, waits for them, and re-layouts  2.32 us
    scatter x1, local copies, waits for them, and re-layouts, on_device(): asks = asks.at[:, 0, 1].set(request_adapter[0].astype(jnp.float32))  1.27 us
  transfers between devices with their start and end apart: 8, of which 3 were waited for; matrix products, arithmetic and copies ran while one was open for 2% of the time, Pallas kernels for 0%

profile of v1, /device:TPU:0, one launch (start us, length us, event | category | flops | bytes accessed | tf_op | source)
XLA Modules:
  0.0 62.1 jit_solution(3182965527065117216)
XLA Ops:
  0.0 0.0 copy-start
  0.8 0.8 %select_reduce_fusion = s32[8]{0:T(128)S(1)} fusion(s32[8]{0:T(128)} %bitcast.124, s32[8]{0:T(128)} %bitcast.125, pred[8]{0:T(512)(128)(4,1)S(1)} %iota_compare_fusion.2), kind=kLoop, calls=%fused_computation.58 | loop fusion | flops 248 | bytes 104 | tf_op jit(solution)/shard_map/reduce_max | solution.py:121
  1.6 0.1 copy.106
  2.3 0.6 slice.88
  2.9 1.1 %copy.123 = bf16[8,8,32,128]{3,2,1,0:T(8,128)(2,1)S(1)} copy(bf16[8,8,32,128]{3,1,2,0:T(8,128)(2,1)} %bitcast.116) | data formatting | bytes 1048576
  4.1 0.0 copy-start.4
  4.1 0.2 copy.104
  4.4 0.6 copy-done.4
  5.0 1.3 %scatter.9 = bf16[8,1,128]{2,1,0:T(2,128)(2,1)S(1)} dynamic-update-slice(bf16[8,1,128]{2,1,0:T(2,128)(2,1)S(1)} %scatter.6, bf16[8,1,1]{2,1,0:T(2,128)(2,1)S(1)} %broadcast.156, s32[]{:T(128)} %constant.108.clone.1, s32[]{:T(128)} %constant.108.clone.1, s32[]{:T(128)} %bitcast.9) | dynamic-update-slice | bytes 36 | tf_op jit(solution)/shard_map/scatter | solution.py:124
  6.4 0.1 constant_dynamic-slice_fusion
  6.4 3.0 %collective-permute-start = (bf16[1,289,128]{2,1,0:T(8,128)(2,1)S(1)}, bf16[1,289,128]{2,1,0:T(8,128)(2,1)S(1)}, u32[]{:S(2)}, u32[]{:S(2)}) collective-permute-start(bf16[1,289,128]{2,1,0:T(8,128)(2,1)S(1)} %get-tuple-element.35), channel_id=1, source_target_pairs={{0,2},{2,0},{4,6},{6,4},{8,10},{10,8},{12,14},{14,12},{1,3},{3,1},... | collective-permute-start | bytes 221960 | tf_op jit(solution)/shard_map/ppermute | solution.py:136
  9.4 1.6 %collective-permute-start.1 = (bf16[1,289,128]{2,1,0:T(8,128)(2,1)S(1)}, bf16[1,289,128]{2,1,0:T(8,128)(2,1)S(1)}, u32[]{:S(2)}, u32[]{:S(2)}) collective-permute-start(bf16[1,289,128]{2,1,0:T(8,128)(2,1)S(1)} %get-tuple-element.34), channel_id=1, source_target_pairs={{0,4},{2,6},{4,0},{6,2},{8,12},{10,14},{12,8},{14,10},{1,5},{3,7},... | collective-permute-start | bytes 221960 | tf_op jit(solution)/shard_map/ppermute | solution.py:136
  11.0 0.0 collective-permute-start.2
  11.0 3.0 %collective-permute-start.3 = (bf16[1,289,128]{2,1,0:T(8,128)(2,1)S(1)}, bf16[1,289,128]{2,1,0:T(8,128)(2,1)S(1)}, u32[]{:S(2)}, u32[]{:S(2)}) collective-permute-start(bf16[1,289,128]{2,1,0:T(8,128)(2,1)S(1)} %get-tuple-element.32), channel_id=1, source_target_pairs={{0,8},{2,10},{4,12},{6,14},{8,0},{10,2},{12,4},{14,6},{1,9},{3,11}... | collective-permute-start | bytes 221960 | tf_op jit(solution)/shard_map/ppermute | solution.py:136
  14.0 1.3 %collective-permute-start.4 = (bf16[1,289,128]{2,1,0:T(8,128)(2,1)S(1)}, bf16[1,289,128]{2,1,0:T(8,128)(2,1)S(1)}, u32[]{:S(2)}, u32[]{:S(2)}) collective-permute-start(bf16[1,289,128]{2,1,0:T(8,128)(2,1)S(1)} %get-tuple-element.31), channel_id=1, source_target_pairs={{0,10},{2,8},{4,14},{6,12},{8,2},{10,0},{12,6},{14,4},{1,11},{3,9}... | collective-permute-start | bytes 221960 | tf_op jit(solution)/shard_map/ppermute | solution.py:136
  15.4 0.1 broadcast_in_dim.83
  15.4 0.1 reshape.235
  15.5 0.0 collective-permute-done
  15.5 3.7 %collective-permute-start.5 = (bf16[1,289,128]{2,1,0:T(8,128)(2,1)S(1)}, bf16[1,289,128]{2,1,0:T(8,128)(2,1)S(1)}, u32[]{:S(2)}, u32[]{:S(2)}) collective-permute-start(bf16[1,289,128]{2,1,0:T(8,128)(2,1)S(1)} %get-tuple-element.30), channel_id=1, source_target_pairs={{0,12},{2,14},{4,8},{6,10},{8,4},{10,6},{12,0},{14,2},{1,13},{3,15... | collective-permute-start | bytes 221960 | tf_op jit(solution)/shard_map/ppermute | solution.py:136
  19.2 0.0 collective-permute-done.1
  19.2 0.1 collective-permute-start.6
  19.3 0.0 collective-permute-done.2
  19.4 0.0 collective-permute-done.3
  19.4 6.1 %collective-permute-done.4 = bf16[1,289,128]{2,1,0:T(8,128)(2,1)S(1)} collective-permute-done((bf16[1,289,128]{2,1,0:T(8,128)(2,1)S(1)}, bf16[1,289,128]{2,1,0:T(8,128)(2,1)S(1)}, u32[]{:S(2)}, u32[]{:S(2)}) %collective-permute-start.4) | collective-permute-done | bytes 74016 | tf_op jit(solution)/shard_map/ppermute | solution.py:136
  25.6 0.0 collective-permute-done.5
  25.6 0.9 %collective-permute-done.6 = bf16[1,289,128]{2,1,0:T(8,128)(2,1)S(1)} collective-permute-done((bf16[1,289,128]{2,1,0:T(8,128)(2,1)S(1)}, bf16[1,289,128]{2,1,0:T(8,128)(2,1)S(1)}, u32[]{:S(2)}, u32[]{:S(2)}) %collective-permute-start.6) | collective-permute-done | bytes 74016 | tf_op jit(solution)/shard_map/ppermute | solution.py:136
  26.5 0.7 %gather_fusion = bf16[8,289,128]{2,1,0:T(8,128)(2,1)S(1)} fusion(bf16[8,289,128]{2,1,0:T(8,128)(2,1)S(1)} %bitcast.114, s32[1024]{0:T(1024)S(1)} %pad_clamp_fusion.2), kind=kCustom, calls=%fused_computation | custom fusion | bytes 1183776 | tf_op jit(solution)/shard_map/gather | solution.py:137
  27.2 0.0 copy-start.3
  27.2 0.1 copy.122
  27.4 0.4 copy.114
  27.7 0.4 copy-done.3
  28.1 0.6 gather_fusion.2
  28.7 0.2 fusion.7
  28.9 0.2 copy.116
  29.1 0.7 %gather_fusion.1 = bf16[8,288,128]{1,2,0:T(8,128)(2,1)S(1)} fusion(bf16[8,288,128]{1,2,0:T(8,128)(2,1)S(1)} %copy.114, s32[1024]{0:T(1024)S(1)} %get-tuple-element.56), kind=kCustom, calls=%fused_computation.1 | custom fusion | bytes 1179680 | tf_op jit(solution)/shard_map/jit(_take)/gather | solution.py:144
  29.8 0.2 broadcast_select_fusion
  30.0 0.2 pad_maximum_fusion
  30.2 1.1 %copy.117 = bf16[8,352,128]{2,1,0:T(8,128)(2,1)} copy(bf16[8,352,128]{1,2,0:T(8,128)(2,1)S(1)} %pad_maximum_fusion) | data formatting | bytes 1441792 | tf_op jit(solution)/shard_map/concatenate | solution.py:147
  31.3 0.0 copy-start.1
  31.3 5.4 %all-to-all-start = ((bf16[8,352,128]{2,1,0:T(8,128)(2,1)}), bf16[8,352,128]{2,1,0:T(8,128)(2,1)S(1)}, u32[]{:S(2)}, u32[]{:S(2)}) async-start(bf16[8,352,128]{2,1,0:T(8,128)(2,1)} %copy.117), calls=%async_computation | async-start | bytes 1441792 | tf_op jit(solution)/shard_map/all_to_all | solution.py:148
  36.8 0.2 broadcast_in_dim.86
  36.9 0.2 broadcast_in_dim.87
  37.1 0.3 copy.121
  37.4 0.0 copy-done.1
  37.5 0.3 multiply_cosine_fusion
  37.8 0.1 fusion.18
  37.9 0.1 fusion.15
  38.0 17.5 %all-to-all-done = bf16[8,352,128]{2,1,0:T(8,128)(2,1)S(1)} async-done(((bf16[8,352,128]{2,1,0:T(8,128)(2,1)}), bf16[8,352,128]{2,1,0:T(8,128)(2,1)S(1)}, u32[]{:S(2)}, u32[]{:S(2)}) %all-to-all-start) | async-done | bytes 720928 | tf_op jit(solution)/shard_map/all_to_all | solution.py:148
  55.5 0.1 copy.118
  55.6 0.0 copy-start.2
  55.6 0.0 copy-done
  55.6 0.5 convolution_bitcast_fusion
  56.1 3.4 %psum.7 = bf16[128,64]{0,1:T(8,128)(2,1)S(1)} all-reduce(f32[128,64]{0,1:T(8,128)S(1)} %convolution_bitcast_fusion), channel_id=1, replica_groups=mesh['parts'=2,'req'=8,'mp'=2] {'mp'}, use_global_device_ids=true, to_apply=%region_1.2 | all-reduce | flops 8192 | bytes 49152 | tf_op jit(solution)/shard_map/psum | solution.py:157
  59.6 0.0 copy-done.2
  59.6 0.2 convolution_add_fusion
  59.8 0.1 reshape.204
  59.9 0.2 slice_negate_fusion
  60.2 0.1 copy.120
  60.4 0.4 fusion.29
  60.9 0.2 fusion.1
  61.0 0.3 convolution_convert_fusion
  61.3 0.7 %reshape.206 = bf16[128,512]{1,0:T(8,128)(2,1)} reshape(bf16[512,128]{1,0:T(8,128)(2,1)S(1)} %convolution_convert_fusion) | data formatting | bytes 262144 | tf_op jit(solution)/shard_map/reshape | solution.py:92
  (43 shorter events, 0.7 us)
Async XLA Ops:
  0.0 55.6 %copy-start = (bf16[128,4096]{1,0:T(8,128)(2,1)S(1)}, bf16[128,4096]{1,0:T(8,128)(2,1)}, u32[]{:S(2)}) copy-start(bf16[128,4096]{1,0:T(8,128)(2,1)} %param.14) | copy-start | bytes 3145732
  4.1 0.8 %copy-start.4 = (bf16[1,1,64,512]{3,2,1,0:T(8,128)(2,1)S(1)}, bf16[1,1,64,512]{3,2,1,0:T(8,128)(2,1)}, u32[]{:S(2)}) copy-start(bf16[1,1,64,512]{3,2,1,0:T(8,128)(2,1)} %param.19) | copy-start | bytes 196612
  6.4 9.1 %collective-permute-start = (bf16[1,289,128]{2,1,0:T(8,128)(2,1)S(1)}, bf16[1,289,128]{2,1,0:T(8,128)(2,1)S(1)}, u32[]{:S(2)}, u32[]{:S(2)}) collective-permute-start(bf16[1,289,128]{2,1,0:T(8,128)(2,1)S(1)} %get-tuple-element.35), channel_id=1, source_target_pairs={{0,2},{2,0},{4,6},{6,4},{8,10},{10,8},{12,14},{14,12},{1,3},{3,1},... | collective-permute-start | bytes 221960 | tf_op jit(solution)/shard_map/ppermute | solution.py:136
  9.4 9.8 %collective-permute-start.1 = (bf16[1,289,128]{2,1,0:T(8,128)(2,1)S(1)}, bf16[1,289,128]{2,1,0:T(8,128)(2,1)S(1)}, u32[]{:S(2)}, u32[]{:S(2)}) collective-permute-start(bf16[1,289,128]{2,1,0:T(8,128)(2,1)S(1)} %get-tuple-element.34), channel_id=1, source_target_pairs={{0,4},{2,6},{4,0},{6,2},{8,12},{10,14},{12,8},{14,10},{1,5},{3,7},... | collective-permute-start | bytes 221960 | tf_op jit(solution)/shard_map/ppermute | solution.py:136
  11.0 8.3 %collective-permute-start.2 = (bf16[1,289,128]{2,1,0:T(8,128)(2,1)S(1)}, bf16[1,289,128]{2,1,0:T(8,128)(2,1)S(1)}, u32[]{:S(2)}, u32[]{:S(2)}) collective-permute-start(bf16[1,289,128]{2,1,0:T(8,128)(2,1)S(1)} %get-tuple-element.33), channel_id=1, source_target_pairs={{0,6},{2,4},{4,2},{6,0},{8,14},{10,12},{12,10},{14,8},{1,7},{3,5},... | collective-permute-start | bytes 221960 | tf_op jit(solution)/shard_map/ppermute | solution.py:136
  11.0 8.3 %collective-permute-start.3 = (bf16[1,289,128]{2,1,0:T(8,128)(2,1)S(1)}, bf16[1,289,128]{2,1,0:T(8,128)(2,1)S(1)}, u32[]{:S(2)}, u32[]{:S(2)}) collective-permute-start(bf16[1,289,128]{2,1,0:T(8,128)(2,1)S(1)} %get-tuple-element.32), channel_id=1, source_target_pairs={{0,8},{2,10},{4,12},{6,14},{8,0},{10,2},{12,4},{14,6},{1,9},{3,11}... | collective-permute-start | bytes 221960 | tf_op jit(solution)/shard_map/ppermute | solution.py:136
  14.0 11.5 %collective-permute-start.4 = (bf16[1,289,128]{2,1,0:T(8,128)(2,1)S(1)}, bf16[1,289,128]{2,1,0:T(8,128)(2,1)S(1)}, u32[]{:S(2)}, u32[]{:S(2)}) collective-permute-start(bf16[1,289,128]{2,1,0:T(8,128)(2,1)S(1)} %get-tuple-element.31), channel_id=1, source_target_pairs={{0,10},{2,8},{4,14},{6,12},{8,2},{10,0},{12,6},{14,4},{1,11},{3,9}... | collective-permute-start | bytes 221960 | tf_op jit(solution)/shard_map/ppermute | solution.py:136
  15.5 10.0 %collective-permute-start.5 = (bf16[1,289,128]{2,1,0:T(8,128)(2,1)S(1)}, bf16[1,289,128]{2,1,0:T(8,128)(2,1)S(1)}, u32[]{:S(2)}, u32[]{:S(2)}) collective-permute-start(bf16[1,289,128]{2,1,0:T(8,128)(2,1)S(1)} %get-tuple-element.30), channel_id=1, source_target_pairs={{0,12},{2,14},{4,8},{6,10},{8,4},{10,6},{12,0},{14,2},{1,13},{3,15... | collective-permute-start | bytes 221960 | tf_op jit(solution)/shard_map/ppermute | solution.py:136
  19.2 7.2 %collective-permute-start.6 = (bf16[1,289,128]{2,1,0:T(8,128)(2,1)S(1)}, bf16[1,289,128]{2,1,0:T(8,128)(2,1)S(1)}, u32[]{:S(2)}, u32[]{:S(2)}) collective-permute-start(bf16[1,289,128]{2,1,0:T(8,128)(2,1)S(1)} %get-tuple-element.29), channel_id=1, source_target_pairs={{0,14},{2,12},{4,10},{6,8},{8,6},{10,4},{12,2},{14,0},{1,15},{3,13... | collective-permute-start | bytes 221960 | tf_op jit(solution)/shard_map/ppermute | solution.py:136
  27.2 1.0 %copy-start.3 = (bf16[16,32,256]{2,1,0:T(8,128)(2,1)S(1)}, bf16[16,32,256]{2,1,0:T(8,128)(2,1)}, u32[]{:S(2)}) copy-start(bf16[16,32,256]{2,1,0:T(8,128)(2,1)} %param.17) | copy-start | bytes 786436
  31.3 6.1 %copy-start.1 = (bf16[128,256]{1,0:T(8,128)(2,1)S(1)}, bf16[128,256]{1,0:T(8,128)(2,1)}, u32[]{:S(2)}) copy-start(bf16[128,256]{1,0:T(8,128)(2,1)} %param.16) | copy-start | bytes 196612
  31.3 24.1 %all-to-all-start = ((bf16[8,352,128]{2,1,0:T(8,128)(2,1)}), bf16[8,352,128]{2,1,0:T(8,128)(2,1)S(1)}, u32[]{:S(2)}, u32[]{:S(2)}) async-start(bf16[8,352,128]{2,1,0:T(8,128)(2,1)} %copy.117), calls=%async_computation | async-start | bytes 1441792 | tf_op jit(solution)/shard_map/all_to_all | solution.py:148
  55.6 4.0 %copy-start.2 = (bf16[128,512]{1,0:T(8,128)(2,1)S(1)}, bf16[128,512]{1,0:T(8,128)(2,1)}, u32[]{:S(2)}) copy-start(bf16[128,512]{1,0:T(8,128)(2,1)} %param.15) | copy-start | bytes 393220
